TPU v7x, 32 devices: a whole 2x2x4 slice. The times are simulated.
32 devices in a mesh: shots: 2 (over y), gx: 4 (over z), gy: 4 (over x, core).
Axes of the slice: x: 2, y: 2, z: 4, core: 2. Of those that a mesh axis runs over, the one named last changes fastest.
Arguments:
- p_now: float32 [64, 64, 128], P(('shots', 'gx'), 'gy'), parts along dimension 0, may hold values from -6 to 6
- q_now: float32 [64, 64, 128], P(('shots', 'gx'), 'gy'), parts along dimension 0, may hold values from -6 to 6
- p_prev: float32 [64, 64, 128], P(('shots', 'gx'), 'gy'), parts along dimension 0, may hold values from -6 to 6
- q_prev: float32 [64, 64, 128], P(('shots', 'gx'), 'gy'), parts along dimension 0, may hold values from -6 to 6
- speed: float32 [32, 64, 128], P('gx', 'gy'), may hold values from 0.05 to 0.2
- epsilon: float32 [32, 64, 128], P('gx', 'gy'), may hold values from 0.05 to 0.35
- delta: float32 [32, 64, 128], P('gx', 'gy'), may hold values from 0 to 0.3
- theta: float32 [32, 64, 128], P('gx', 'gy'), may hold values from -1 to 1
- phi: float32 [32, 64, 128], P('gx', 'gy'), may hold values from -3.140625 to 3.140625
- snapshots: bfloat16 [2, 64, 64, 128], P(None, ('shots', 'gx'), 'gy'), parts along dimension 1, may hold values from -6 to 6
- traces: float32 [1024, 4096], P(None, ('shots', 'gx', 'gy')), parts along dimension 1, may hold values from -6 to 6
- time_steps: int32 [4], P('shots'), parts along dimension 0, may hold values from 0 to 1023
- rec_owner: int32 [4096, 1], P(('shots', 'gx', 'gy')), parts along dimension 0, may hold values from 0 to 3; in each aligned block of 128 rows (0 to 127, 128 to 255, ...) at most 64 rows name the same one
- rec_local: int32 [4096], P(('shots', 'gx', 'gy')), parts along dimension 0, may hold values from 0 to 16383
Outputs:
- p_next: float32 [64, 64, 128], P(('shots', 'gx'), 'gy'), parts along dimension 0
- q_next: float32 [64, 64, 128], P(('shots', 'gx'), 'gy'), parts along dimension 0
- p_mid: float32 [64, 64, 128], P(('shots', 'gx'), 'gy'), parts along dimension 0
- q_mid: float32 [64, 64, 128], P(('shots', 'gx'), 'gy'), parts along dimension 0
- image: float32 [64, 64, 128], P(('shots', 'gx'), 'gy'), parts along dimension 0
There are 2 independent parts, one for each index of `shots`. A program takes and returns all parts, laid end to end along the dimension named above; an argument that names none is the same for every part. Nothing has to cross between parts.
Inputs may be any that keep to these rules, and one draw needn't show every extreme that they name: `rec_owner`: the 128 receivers of one device (aligned blocks of 128 rows) name any one owner at most 64 times, a bound that some block reaches. `rec_local`: A receiver's cell lies in the band of the second dimension that the device holding the receiver covers.
All inputs are finite; a program needn't handle non-finite values.
Results may differ from a plain program's by a relative error of at most 0.0003.
Values sent between devices are 32-bit elements; how exact they have to be, the bound alone decides.
No kernel may reach another device: no remote copies, remote signals or barrier semaphores. Data moves between devices by JAX's collectives and lax.ppermute only.
A program may use at most 64 MiB of HBM per device.

v0:
```python
import jax
import jax.numpy as jnp
from jax import lax
from jax.sharding import PartitionSpec as P

second_coef = (-205.0 / 72.0, 8.0 / 5.0, -1.0 / 5.0, 8.0 / 315.0, -1.0 / 560.0)
first_coef = (4.0 / 5.0, -1.0 / 5.0, 4.0 / 105.0, -1.0 / 280.0)


def padded_2(cells, sides, width):
    for axis, dim in sides:
        count = lax.axis_size(axis)
        ends = count - 1
        head = lax.slice_in_dim(cells, 0, width, axis=dim)
        tail = lax.slice_in_dim(cells, cells.shape[dim] - width, cells.shape[dim], axis=dim)
        cells = jnp.concatenate(
            [
                lax.ppermute(tail, axis, [(i, (i + 1) % count) for i in range(ends)]),
                cells,
                lax.ppermute(head, axis, [((i + 1) % count, i) for i in range(ends)]),
            ],
            axis=dim,
        )
    return cells


def derivatives(padded, sx, sy, sz):

    def part(dx, dy, dz):
        return padded[:, 4 + dx : 4 + dx + sx, 4 + dy : 4 + dy + sy, 4 + dz : 4 + dz + sz]

    centre = part(0, 0, 0)
    dxx = second_coef[0] * centre
    dyy = second_coef[0] * centre
    dzz = second_coef[0] * centre
    for k in range(1, 5):
        dxx = dxx + second_coef[k] * (part(k, 0, 0) + part(-k, 0, 0))
        dyy = dyy + second_coef[k] * (part(0, k, 0) + part(0, -k, 0))
        dzz = dzz + second_coef[k] * (part(0, 0, k) + part(0, 0, -k))
    dy_wide = 0.0
    dz_xwide = 0.0
    dz_ywide = 0.0
    for k in range(1, 5):
        weight = first_coef[k - 1]
        dy_wide = dy_wide + weight * (
            padded[:, :, 4 + k : 4 + k + sy, 4 : 4 + sz]
            - padded[:, :, 4 - k : 4 - k + sy, 4 : 4 + sz]
        )
        dz_xwide = dz_xwide + weight * (
            padded[:, :, 4 : 4 + sy, 4 + k : 4 + k + sz]
            - padded[:, :, 4 : 4 + sy, 4 - k : 4 - k + sz]
        )
        dz_ywide = dz_ywide + weight * (
            padded[:, 4 : 4 + sx, :, 4 + k : 4 + k + sz]
            - padded[:, 4 : 4 + sx, :, 4 - k : 4 - k + sz]
        )
    dxy = 0.0
    dxz = 0.0
    dyz = 0.0
    for k in range(1, 5):
        weight = first_coef[k - 1]
        dxy = dxy + weight * (dy_wide[:, 4 + k : 4 + k + sx] - dy_wide[:, 4 - k : 4 - k + sx])
        dxz = dxz + weight * (dz_xwide[:, 4 + k : 4 + k + sx] - dz_xwide[:, 4 - k : 4 - k + sx])
        dyz = dyz + weight * (
            dz_ywide[:, :, 4 + k : 4 + k + sy] - dz_ywide[:, :, 4 - k : 4 - k + sy]
        )
    return (centre, dxx, dyy, dzz, dxy, dxz, dyz)


def advance(padded, previous, speed, epsilon, delta, theta, phi, source):
    sx, sy, sz = (previous.shape[1], previous.shape[2], previous.shape[3])
    centre, dxx, dyy, dzz, dxy, dxz, dyz = derivatives(padded, sx, sy, sz)
    axis_x = jnp.sin(theta) * jnp.cos(phi)
    axis_y = jnp.sin(theta) * jnp.sin(phi)
    axis_z = jnp.cos(theta)
    rotated = (
        axis_x * axis_x * dxx
        + axis_y * axis_y * dyy
        + axis_z * axis_z * dzz
        + 2.0 * axis_x * axis_y * dxy
        + 2.0 * axis_x * axis_z * dxz
        + 2.0 * axis_y * axis_z * dyz
    )
    remainder = dxx + dyy + dzz - rotated
    root_delta = jnp.sqrt(1.0 + 2.0 * delta)
    p_new = (
        2.0 * centre[0]
        - previous[0]
        + speed * ((1.0 + 2.0 * epsilon) * remainder[0] + root_delta * rotated[1])
        + source
    )
    q_new = (
        2.0 * centre[1] - previous[1] + speed * (root_delta * remainder[0] + rotated[1]) + source
    )
    return jnp.stack([p_new, q_new])


def pad_depth(fields):
    return jnp.pad(fields, ((0, 0), (0, 0), (0, 0), (4, 4)))


def widened(fields):
    return pad_depth(padded_2(fields, (("gx", 1), ("gy", 2)), 4))


def local(
    p_now,
    q_now,
    p_prev,
    q_prev,
    speed,
    epsilon,
    delta,
    theta,
    phi,
    snapshots,
    traces,
    time_steps,
    rec_owner,
    rec_local,
):
    sx, sy, sz = p_now.shape
    cells = sx * sy * sz
    groups = lax.axis_size("gx")
    held = rec_local.shape[0]
    samples = jnp.take(traces, time_steps, axis=0)
    owner = rec_owner[:, 0]
    capacity = 2 * held // groups
    onehot = (owner[:, None] == jnp.arange(groups, dtype=jnp.int32)[None, :]).astype(jnp.int32)
    running = jnp.cumsum(onehot, axis=0)
    rank = jnp.sum(onehot * running, axis=1) - 1
    position = owner * capacity + rank
    payload = jnp.concatenate([samples, rec_local.astype(jnp.float32)[None, :]], axis=0)
    slots = jnp.zeros((3, groups * capacity), jnp.float32).at[:, position].set(payload)
    slots = slots.reshape(3, groups, capacity)
    arrived = lax.all_to_all(slots, "gx", split_axis=1, concat_axis=1, tiled=True)
    values = arrived[0:2].reshape(2, groups * capacity)
    target = arrived[2].reshape(groups * capacity).astype(jnp.int32)
    sources = jnp.zeros((2, cells), jnp.float32).at[:, target].add(values).reshape(2, sx, sy, sz)
    current = jnp.stack([p_now, q_now])
    earlier = jnp.stack([p_prev, q_prev])
    middle = advance(widened(current), earlier, speed, epsilon, delta, theta, phi, sources[0])
    final = advance(widened(middle), current, speed, epsilon, delta, theta, phi, sources[1])
    image = (
        snapshots[0].astype(jnp.float32) * middle[0] + snapshots[1].astype(jnp.float32) * final[0]
    )
    return (final[0], final[1], middle[0], middle[1], image)


def solution(mesh):
    return jax.shard_map(
        local,
        mesh=mesh,
        in_specs=(
            P(("shots", "gx"), "gy", None),
            P(("shots", "gx"), "gy", None),
            P(("shots", "gx"), "gy", None),
            P(("shots", "gx"), "gy", None),
            P("gx", "gy", None),
            P("gx", "gy", None),
            P("gx", "gy", None),
            P("gx", "gy", None),
            P("gx", "gy", None),
            P(None, ("shots", "gx"), "gy", None),
            P(None, ("shots", "gx", "gy")),
            P("shots"),
            P(("shots", "gx", "gy"), None),
            P(("shots", "gx", "gy")),
        ),
        out_specs=(
            P(("shots", "gx"), "gy", None),
            P(("shots", "gx"), "gy", None),
            P(("shots", "gx"), "gy", None),
            P(("shots", "gx"), "gy", None),
            P(("shots", "gx"), "gy", None),
        ),
        check_vma=False,
    )
```

profile of v0, /device:TPU:18, one launch (start us, length us, event | category | flops | bytes accessed | tf_op | source)
XLA Modules:
  0.0 71.5 jit_solution(5272176775762559091)
XLA Ops:
  0.6 0.0 copy-start
  0.6 0.7 %compare_select_fusion.1 = s32[2]{0:T(128)S(1)} fusion(s32[2]{0:T(128)} %param.25), kind=kLoop, calls=%fused_computation.299 | loop fusion | flops 6 | bytes 16 | tf_op jit(solution)/shard_map/jit(_take)/jit(_where)/select_n | solution.py:126
  1.4 0.7 compare_and_fusion
  2.0 0.7 %fusion.156 = s32[128,4]{1,0:T(8,128)S(1)} fusion(s32[128]{0:T(128)} %bitcast.80), kind=kLoop, calls=%fused_computation.286 | loop fusion | flops 1024 | bytes 2560 | tf_op jit(solution)/shard_map/convert_element_type | solution.py:129
  2.8 0.2 reduce_window_sum.11
  2.9 0.8 %select_reduce_fusion = s32[128]{0:T(128)S(1)} fusion(s32[128,4]{1,0:T(8,128)S(1)} %reduce_window_sum.11, s32[128]{0:T(128)} %bitcast.81), kind=kLoop, calls=%fused_computation.284 | loop fusion | flops 1408 | bytes 3072 | tf_op jit(solution)/shard_map/reduce_sum | solution.py:131
  3.8 0.7 fusion.160
  4.4 0.7 convert_bitcast_fusion
  5.1 0.6 gather_fusion
  5.7 0.1 broadcast_select_fusion
  5.8 0.1 copy.25
  5.9 0.9 %scatter_custom_fusion = f32[3,256]{0,1:T(8,128)S(1)} fusion(s32[128]{0:T(128)S(1)} %fusion.160, f32[128,3]{1,0:T(8,128)S(1)} %copy.25, f32[]{:T(128)} %constant.26.clone.1), kind=kCustom, calls=%fused_computation.287 | custom fusion | bytes 3076 | tf_op jit(solution)/shard_map/scatter | solution.py:134
  6.8 0.1 copy.26
  6.9 0.7 reshape.111
  7.6 5.2 %all-to-all-start = ((f32[4,1,192]{2,1,0:T(1,128)}), f32[4,1,192]{2,1,0:T(1,128)S(1)}, u32[]{:S(2)}, u32[]{:S(2)}) async-start(f32[4,1,192]{2,1,0:T(1,128)} %reshape.111), calls=%async_computation | async-start | bytes 8192 | tf_op jit(solution)/shard_map/all_to_all | solution.py:136
  12.8 0.8 %fusion.152 = (f32[2,4,16,128]{3,2,1,0:T(8,128)S(1)}, f32[2,4,16,128]{3,2,1,0:T(8,128)S(1)}) fusion(f32[1,8,16,128]{3,2,1,0:T(8,128)} %bitcast.59, f32[1,8,16,128]{3,2,1,0:T(8,128)} %bitcast.47), kind=kLoop, calls=%fused_computation.259 | loop fusion | flops 32768 | bytes 262144 | tf_op jit(solution)/shard_map/stack | solution.py:140
  13.6 2.5 %collective-permute-start = (f32[2,4,16,128]{3,2,1,0:T(8,128)S(1)}, f32[2,4,16,128]{3,2,1,0:T(8,128)S(1)}, u32[]{:S(2)}, u32[]{:S(2)}) collective-permute-start(f32[2,4,16,128]{3,2,1,0:T(8,128)S(1)} %get-tuple-element.42), channel_id=1, source_target_pairs={{4,0},{8,4},{12,8},{5,1},{9,5},{13,9},{6,2},{10,6},{14,10},{7,3},{... | collective-permute-start | bytes 196616 | tf_op jit(solution)/shard_map/ppermute | solution.py:20
  16.1 3.4 %collective-permute-start.1 = (f32[2,4,16,128]{3,2,1,0:T(8,128)S(1)}, f32[2,4,16,128]{3,2,1,0:T(8,128)S(1)}, u32[]{:S(2)}, u32[]{:S(2)}) collective-permute-start(f32[2,4,16,128]{3,2,1,0:T(8,128)S(1)} %get-tuple-element.41), channel_id=1, source_target_pairs={{0,4},{4,8},{8,12},{1,5},{5,9},{9,13},{2,6},{6,10},{10,14},{3,7},{... | collective-permute-start | bytes 196616 | tf_op jit(solution)/shard_map/ppermute | solution.py:18
  19.4 1.1 %fusion.171 = (f32[8,16,128]{2,1,0:T(8,128)S(1)}, f32[8,16,128]{2,1,0:T(8,128)S(1)}) fusion(f32[8,16,128]{2,1,0:T(8,128)} %param.21), kind=kLoop, calls=%fused_computation.311 | loop fusion | bytes 196608 | tf_op jit(solution)/shard_map/sin | solution.py:73
  20.5 1.1 %fusion.161 = (f32[8,16,128]{2,1,0:T(8,128)S(1)}, f32[8,16,128]{2,1,0:T(8,128)S(1)}, f32[8,16,128]{2,1,0:T(8,128)S(1)}, f32[8,16,128]{2,1,0:T(8,128)S(1)}, f32[8...) fusion(f32[8,16,128]{2,1,0:T(8,128)S(1)} %get-tuple-element.44, f32[8,16,128]{2,1,0:T(8,128)} %param.22, ...), kind=kLoop, calls=%fused_computation.309 | loop fusion | flops 163840 | bytes 589824 | tf_op jit(solution)/shard_map/mul | solution.py:77
  21.6 0.0 all-to-all-done
  21.6 0.5 broadcast.301
  22.2 0.7 reduce.8
  22.8 0.1 reshape.112
  22.9 0.1 convert_element_type.37
  23.0 0.1 reshape.90
  23.1 0.1 copy.28
  23.3 5.1 %scatter_custom_fusion.1 = f32[2,16384]{0,1:T(8,128)} fusion(s32[256]{0:T(256)S(1)} %bitcast.82, f32[256,2]{1,0:T(8,128)S(1)} %copy.28, f32[]{:T(128)} %constant.26.clone.1), kind=kCustom, calls=%fused_computation.5 | custom fusion | flops 512 | bytes 131076 | tf_op jit(solution)/shard_map/scatter-add | solution.py:139
  28.4 12.3 %slice_reduce_fusion.1 = (f32[16384]{0:T(1024)S(1)}, f32[16384]{0:T(1024)S(1)}) fusion(f32[2,16384]{0,1:T(8,128)} %scatter_custom_fusion.1), kind=kLoop, calls=%fused_computation.4 | loop fusion | bytes 262144 | tf_op jit(solution)/shard_map/slice | solution.py:142
  40.7 0.0 collective-permute-done.1
  40.8 1.9 %collective-permute-start.2 = (f32[2,16,4,128]{3,2,1,0:T(4,128)S(1)}, f32[2,16,4,128]{3,2,1,0:T(4,128)S(1)}, u32[]{:S(2)}, u32[]{:S(2)}) collective-permute-start(f32[2,16,4,128]{3,2,1,0:T(4,128)S(1)} %get-tuple-element.27), channel_id=1, source_target_pairs={{1,0},{2,1},{3,2},{5,4},{6,5},{7,6},{9,8},{10,9},{11,10},{13,12},{... | collective-permute-start | bytes 196616 | tf_op jit(solution)/shard_map/ppermute | solution.py:20
  42.7 0.0 copy-start.5
  42.7 0.0 copy-start.6
  42.7 0.0 copy-start.8
  42.8 2.5 %collective-permute-start.3 = (f32[2,16,4,128]{3,2,1,0:T(4,128)S(1)}, f32[2,16,4,128]{3,2,1,0:T(4,128)S(1)}, u32[]{:S(2)}, u32[]{:S(2)}) collective-permute-start(f32[2,16,4,128]{3,2,1,0:T(4,128)S(1)} %get-tuple-element.26), channel_id=1, source_target_pairs={{0,1},{1,2},{2,3},{4,5},{5,6},{6,7},{8,9},{9,10},{10,11},{12,13},{... | collective-permute-start | bytes 196616 | tf_op jit(solution)/shard_map/ppermute | solution.py:18
  45.3 0.0 copy-start.7
  45.4 0.0 copy-start.9
  45.4 0.0 collective-permute-done.2
  45.4 3.1 %collective-permute-done.3 = f32[2,16,4,128]{3,2,1,0:T(4,128)S(1)} collective-permute-done((f32[2,16,4,128]{3,2,1,0:T(4,128)S(1)}, f32[2,16,4,128]{3,2,1,0:T(4,128)S(1)}, u32[]{:S(2)}, u32[]{:S(2)}) %collective-permute-start.3) | collective-permute-done | bytes 65568 | tf_op jit(solution)/shard_map/ppermute | solution.py:18
  48.5 0.4 select_maximum_fusion.5
  48.9 0.4 fusion.39
  49.3 0.1 pad_maximum_fusion
  49.4 0.7 fusion.18
  50.1 0.6 fusion.101
  50.7 0.1 add_add_fusion.2
  50.7 0.0 copy-start.2
  50.8 0.1 add_add_fusion.3
  50.8 0.0 copy-start.4
  50.9 3.1 %collective-permute-start.4 = (f32[2,4,16,128]{3,2,1,0:T(8,128)S(1)}, f32[2,4,16,128]{3,2,1,0:T(8,128)S(1)}, u32[]{:S(2)}, u32[]{:S(2)}) collective-permute-start(f32[2,4,16,128]{3,2,1,0:T(8,128)S(1)} %get-tuple-element.33), channel_id=1, source_target_pairs={{4,0},{8,4},{12,8},{5,1},{9,5},{13,9},{6,2},{10,6},{14,10},{7,3},{... | collective-permute-start | bytes 196616 | tf_op jit(solution)/shard_map/ppermute | solution.py:20
  54.0 2.7 %collective-permute-start.5 = (f32[2,4,16,128]{3,2,1,0:T(8,128)S(1)}, f32[2,4,16,128]{3,2,1,0:T(8,128)S(1)}, u32[]{:S(2)}, u32[]{:S(2)}) collective-permute-start(f32[2,4,16,128]{3,2,1,0:T(8,128)S(1)} %get-tuple-element.32), channel_id=1, source_target_pairs={{0,4},{4,8},{8,12},{1,5},{5,9},{9,13},{2,6},{6,10},{10,14},{3,7},{... | collective-permute-start | bytes 196616 | tf_op jit(solution)/shard_map/ppermute | solution.py:18
  56.7 0.3 collective-permute-done.4
  57.0 3.1 %collective-permute-done.5 = f32[2,4,16,128]{3,2,1,0:T(8,128)S(1)} collective-permute-done((f32[2,4,16,128]{3,2,1,0:T(8,128)S(1)}, f32[2,4,16,128]{3,2,1,0:T(8,128)S(1)}, u32[]{:S(2)}, u32[]{:S(2)}) %collective-permute-start.5) | collective-permute-done | bytes 65568 | tf_op jit(solution)/shard_map/ppermute | solution.py:18
  60.2 1.9 %collective-permute-start.6 = (f32[2,16,4,128]{3,2,1,0:T(4,128)S(1)}, f32[2,16,4,128]{3,2,1,0:T(4,128)S(1)}, u32[]{:S(2)}, u32[]{:S(2)}) collective-permute-start(f32[2,16,4,128]{3,2,1,0:T(4,128)S(1)} %get-tuple-element.23), channel_id=1, source_target_pairs={{1,0},{2,1},{3,2},{5,4},{6,5},{7,6},{9,8},{10,9},{11,10},{13,12},{... | collective-permute-start | bytes 196616 | tf_op jit(solution)/shard_map/ppermute | solution.py:20
  62.1 0.0 copy-start.10
  62.1 2.5 %collective-permute-start.7 = (f32[2,16,4,128]{3,2,1,0:T(4,128)S(1)}, f32[2,16,4,128]{3,2,1,0:T(4,128)S(1)}, u32[]{:S(2)}, u32[]{:S(2)}) collective-permute-start(f32[2,16,4,128]{3,2,1,0:T(4,128)S(1)} %get-tuple-element.22), channel_id=1, source_target_pairs={{0,1},{1,2},{2,3},{4,5},{5,6},{6,7},{8,9},{9,10},{10,11},{12,13},{... | collective-permute-start | bytes 196616 | tf_op jit(solution)/shard_map/ppermute | solution.py:18
  64.7 3.1 %collective-permute-done.7 = f32[2,16,4,128]{3,2,1,0:T(4,128)S(1)} collective-permute-done((f32[2,16,4,128]{3,2,1,0:T(4,128)S(1)}, f32[2,16,4,128]{3,2,1,0:T(4,128)S(1)}, u32[]{:S(2)}, u32[]{:S(2)}) %collective-permute-start.7) | collective-permute-done | bytes 65568 | tf_op jit(solution)/shard_map/ppermute | solution.py:18
  67.8 0.4 select_maximum_fusion
  68.2 0.4 fusion.32
  68.7 0.5 fusion.4
  69.2 0.1 pad_maximum_fusion.1
  69.3 0.2 fusion.11
  69.5 0.6 fusion.50
  70.1 0.7 %fusion.155 = (f32[8,16,128]{2,1,0:T(8,128)}, f32[8,16,128]{2,1,0:T(8,128)}, f32[8,16,128]{2,1,0:T(8,128)S(1)}) fusion(f32[8,16,128]{2,1,0:T(8,128)S(1)} %add_add_fusion.3, bf16[2,8,16,128]{3,2,1,0:T(8,128)(2,1)S(1)} %copy-done.10, f32[8,16,128]{2,1,0:T(8,128)S(1)} %bitcast.73, f32[8,16,128]{2,1,0:T(8,128)S(1)} %copy-done.5, ...), kind=kLoop, calls=%fused_computation.279 | loop fusion | flops 327680 | bytes 983040 | tf_op jit(solution)/shard_map/add | solution.py:145
  70.8 0.7 add_add_fusion
  (26 shorter events, 0.2 us)
Async XLA Ops:
  0.6 4.5 %copy-start = (f32[1024,128]{1,0:T(8,128)S(1)}, f32[1024,128]{1,0:T(8,128)}, u32[]{:S(2)}) copy-start(f32[1024,128]{1,0:T(8,128)} %param.24) | copy-start | bytes 1572868
  7.6 14.1 %all-to-all-start = ((f32[4,1,192]{2,1,0:T(1,128)}), f32[4,1,192]{2,1,0:T(1,128)S(1)}, u32[]{:S(2)}, u32[]{:S(2)}) async-start(f32[4,1,192]{2,1,0:T(1,128)} %reshape.111), calls=%async_computation | async-start | bytes 8192 | tf_op jit(solution)/shard_map/all_to_all | solution.py:136
  13.6 27.1 %collective-permute-start = (f32[2,4,16,128]{3,2,1,0:T(8,128)S(1)}, f32[2,4,16,128]{3,2,1,0:T(8,128)S(1)}, u32[]{:S(2)}, u32[]{:S(2)}) collective-permute-start(f32[2,4,16,128]{3,2,1,0:T(8,128)S(1)} %get-tuple-element.42), channel_id=1, source_target_pairs={{4,0},{8,4},{12,8},{5,1},{9,5},{13,9},{6,2},{10,6},{14,10},{7,3},{... | collective-permute-start | bytes 196616 | tf_op jit(solution)/shard_map/ppermute | solution.py:20
  16.1 24.7 %collective-permute-start.1 = (f32[2,4,16,128]{3,2,1,0:T(8,128)S(1)}, f32[2,4,16,128]{3,2,1,0:T(8,128)S(1)}, u32[]{:S(2)}, u32[]{:S(2)}) collective-permute-start(f32[2,4,16,128]{3,2,1,0:T(8,128)S(1)} %get-tuple-element.41), channel_id=1, source_target_pairs={{0,4},{4,8},{8,12},{1,5},{5,9},{9,13},{2,6},{6,10},{10,14},{3,7},{... | collective-permute-start | bytes 196616 | tf_op jit(solution)/shard_map/ppermute | solution.py:18
  28.4 12.3 %copy-start.1 = (f32[8,16,128]{2,1,0:T(8,128)S(1)}, f32[8,16,128]{2,1,0:T(8,128)}, u32[]{:S(2)}) copy-start(f32[8,16,128]{2,1,0:T(8,128)} %param.15) | copy-start | bytes 196612
  28.4 12.3 %copy-start.3 = (f32[8,16,128]{2,1,0:T(8,128)S(1)}, f32[8,16,128]{2,1,0:T(8,128)}, u32[]{:S(2)}) copy-start(f32[8,16,128]{2,1,0:T(8,128)} %param.14) | copy-start | bytes 196612
  40.8 4.6 %collective-permute-start.2 = (f32[2,16,4,128]{3,2,1,0:T(4,128)S(1)}, f32[2,16,4,128]{3,2,1,0:T(4,128)S(1)}, u32[]{:S(2)}, u32[]{:S(2)}) collective-permute-start(f32[2,16,4,128]{3,2,1,0:T(4,128)S(1)} %get-tuple-element.27), channel_id=1, source_target_pairs={{1,0},{2,1},{3,2},{5,4},{6,5},{7,6},{9,8},{10,9},{11,10},{13,12},{... | collective-permute-start | bytes 196616 | tf_op jit(solution)/shard_map/ppermute | solution.py:20
  42.7 7.9 %copy-start.5 = (f32[8,16,128]{2,1,0:T(8,128)S(1)}, f32[8,16,128]{2,1,0:T(8,128)}, u32[]{:S(2)}) copy-start(f32[8,16,128]{2,1,0:T(8,128)} %param.18) | copy-start | bytes 196612
  42.7 7.9 %copy-start.6 = (f32[8,16,128]{2,1,0:T(8,128)S(1)}, f32[8,16,128]{2,1,0:T(8,128)}, u32[]{:S(2)}) copy-start(f32[8,16,128]{2,1,0:T(8,128)} %param.20) | copy-start | bytes 196612
  42.7 7.9 %copy-start.8 = (f32[8,16,128]{2,1,0:T(8,128)S(1)}, f32[8,16,128]{2,1,0:T(8,128)}, u32[]{:S(2)}) copy-start(f32[8,16,128]{2,1,0:T(8,128)} %param.17) | copy-start | bytes 196612
  42.8 5.7 %collective-permute-start.3 = (f32[2,16,4,128]{3,2,1,0:T(4,128)S(1)}, f32[2,16,4,128]{3,2,1,0:T(4,128)S(1)}, u32[]{:S(2)}, u32[]{:S(2)}) collective-permute-start(f32[2,16,4,128]{3,2,1,0:T(4,128)S(1)} %get-tuple-element.26), channel_id=1, source_target_pairs={{0,1},{1,2},{2,3},{4,5},{5,6},{6,7},{8,9},{9,10},{10,11},{12,13},{... | collective-permute-start | bytes 196616 | tf_op jit(solution)/shard_map/ppermute | solution.py:18
  45.3 5.4 %copy-start.7 = (f32[8,16,128]{2,1,0:T(8,128)S(1)}, f32[8,16,128]{2,1,0:T(8,128)}, u32[]{:S(2)}) copy-start(f32[8,16,128]{2,1,0:T(8,128)} %param.19) | copy-start | bytes 196612
  45.4 5.4 %copy-start.9 = (f32[8,16,128]{2,1,0:T(8,128)S(1)}, f32[8,16,128]{2,1,0:T(8,128)}, u32[]{:S(2)}) copy-start(f32[8,16,128]{2,1,0:T(8,128)} %param.16) | copy-start | bytes 196612
  50.7 20.1 %copy-start.2 = (f32[8,16,128]{2,1,0:T(8,128)}, f32[8,16,128]{2,1,0:T(8,128)S(1)}, u32[]{:S(2)}) copy-start(f32[8,16,128]{2,1,0:T(8,128)S(1)} %get-tuple-element.14) | copy-start | bytes 196612
  50.8 19.2 %copy-start.4 = (f32[8,16,128]{2,1,0:T(8,128)}, f32[8,16,128]{2,1,0:T(8,128)S(1)}, u32[]{:S(2)}) copy-start(f32[8,16,128]{2,1,0:T(8,128)S(1)} %add_add_fusion.3) | copy-start | bytes 196612
  50.9 6.2 %collective-permute-start.4 = (f32[2,4,16,128]{3,2,1,0:T(8,128)S(1)}, f32[2,4,16,128]{3,2,1,0:T(8,128)S(1)}, u32[]{:S(2)}, u32[]{:S(2)}) collective-permute-start(f32[2,4,16,128]{3,2,1,0:T(8,128)S(1)} %get-tuple-element.33), channel_id=1, source_target_pairs={{4,0},{8,4},{12,8},{5,1},{9,5},{13,9},{6,2},{10,6},{14,10},{7,3},{... | collective-permute-start | bytes 196616 | tf_op jit(solution)/shard_map/ppermute | solution.py:20
  54.0 6.2 %collective-permute-start.5 = (f32[2,4,16,128]{3,2,1,0:T(8,128)S(1)}, f32[2,4,16,128]{3,2,1,0:T(8,128)S(1)}, u32[]{:S(2)}, u32[]{:S(2)}) collective-permute-start(f32[2,4,16,128]{3,2,1,0:T(8,128)S(1)} %get-tuple-element.32), channel_id=1, source_target_pairs={{0,4},{4,8},{8,12},{1,5},{5,9},{9,13},{2,6},{6,10},{10,14},{3,7},{... | collective-permute-start | bytes 196616 | tf_op jit(solution)/shard_map/ppermute | solution.py:18
  60.2 4.5 %collective-permute-start.6 = (f32[2,16,4,128]{3,2,1,0:T(4,128)S(1)}, f32[2,16,4,128]{3,2,1,0:T(4,128)S(1)}, u32[]{:S(2)}, u32[]{:S(2)}) collective-permute-start(f32[2,16,4,128]{3,2,1,0:T(4,128)S(1)} %get-tuple-element.23), channel_id=1, source_target_pairs={{1,0},{2,1},{3,2},{5,4},{6,5},{7,6},{9,8},{10,9},{11,10},{13,12},{... | collective-permute-start | bytes 196616 | tf_op jit(solution)/shard_map/ppermute | solution.py:20
  62.1 8.0 %copy-start.10 = (bf16[2,8,16,128]{3,2,1,0:T(8,128)(2,1)S(1)}, bf16[2,8,16,128]{3,2,1,0:T(8,128)(2,1)}, u32[]{:S(2)}) copy-start(bf16[2,8,16,128]{3,2,1,0:T(8,128)(2,1)} %param.23) | copy-start | bytes 196612
  62.1 5.7 %collective-permute-start.7 = (f32[2,16,4,128]{3,2,1,0:T(4,128)S(1)}, f32[2,16,4,128]{3,2,1,0:T(4,128)S(1)}, u32[]{:S(2)}, u32[]{:S(2)}) collective-permute-start(f32[2,16,4,128]{3,2,1,0:T(4,128)S(1)} %get-tuple-element.22), channel_id=1, source_target_pairs={{0,1},{1,2},{2,3},{4,5},{5,6},{6,7},{8,9},{9,10},{10,11},{12,13},{... | collective-permute-start | bytes 196616 | tf_op jit(solution)/shard_map/ppermute | solution.py:18
where the time goes:
time: 72.1 us; the launch traced here: 71.5 us
  starting transfers between devices  25.8 us (36%)
  other arithmetic  18.3 us (25%)
  local copies, waits for them, and re-layouts  16.7 us (23%)
  waiting for transfers between devices  9.66 us (13%)
  between operations  1.04 us (1%)
    slice x1, local copies, waits for them, and re-layouts, local(): sources[0]  12.3 us
    ppermute x4, starting transfers between devices, padded_2(): lax.ppermute(tail, axis, [(i, (i + 1) % count) for i in range(ends)])  11.2 us
    ppermute x4, starting transfers between devices, padded_2(): lax.ppermute(head, axis, [((i + 1) % count, i) for i in range(ends)])  9.42 us
    ppermute x4, waiting for transfers between devices, padded_2(): lax.ppermute(tail, axis, [(i, (i + 1) % count) for i in range(ends)])  9.35 us
    all_to_all x1, starting transfers between devices, local(): lax.all_to_all(slots, 'gx', split_axis=1, concat_axis=1, tiled=True)  5.2 us
    scatter-add x1, other arithmetic, local(): jnp.zeros((2, cells), jnp.float32).at[:, target].add(values)  5.14 us
  transfers between devices with their start and end apart: 9, of which 4 were waited for; matrix products, arithmetic and copies ran while one was open for 31% of the time, Pallas kernels for 0%

commit v1 on v0

--- a/solution.py
+++ b/solution.py
@@ -1,10 +1,40 @@
+import functools
 import jax
 import jax.numpy as jnp
 from jax import lax
 from jax.sharding import PartitionSpec as P
+from jax.lax import axis_index, axis_size, ppermute
 
 second_coef = (-205.0 / 72.0, 8.0 / 5.0, -1.0 / 5.0, 8.0 / 315.0, -1.0 / 560.0)
 first_coef = (4.0 / 5.0, -1.0 / 5.0, 4.0 / 105.0, -1.0 / 280.0)
+
+
+def _press_racks(xin, dim_at, array_axis):
+    aux, view_out = (axis_size("gx"), axis_index("gx"))
+    ready = list(xin.shape)
+    shaped = xin.shape[dim_at] // aux
+    ready[dim_at] = shaped
+    r_now = ready[array_axis]
+    ready[array_axis] = r_now * aux
+    before = jnp.zeros(ready, xin.dtype)
+    b = 0
+    while b < aux:
+        k_now = lax.dynamic_slice_in_dim(xin, (view_out ^ b) * shaped, shaped, axis=dim_at)
+        if b:
+            sheets = []
+            p = 0
+            while p < aux:
+                sheets.append((p, p ^ b))
+                p = p + 1
+            k_now = ppermute(k_now, "gx", sheets)
+        before = lax.dynamic_update_slice_in_dim(
+            before, k_now, (view_out ^ b) * r_now, axis=array_axis
+        )
+        b = b + 1
+    return before
+
+
+space_arrange = functools.partial(_press_racks, dim_at=1, array_axis=1)
 
 
 def padded_2(cells, sides, width):
@@ -133,7 +163,7 @@
     payload = jnp.concatenate([samples, rec_local.astype(jnp.float32)[None, :]], axis=0)
     slots = jnp.zeros((3, groups * capacity), jnp.float32).at[:, position].set(payload)
     slots = slots.reshape(3, groups, capacity)
-    arrived = lax.all_to_all(slots, "gx", split_axis=1, concat_axis=1, tiled=True)
+    arrived = space_arrange(slots)
     values = arrived[0:2].reshape(2, groups * capacity)
     target = arrived[2].reshape(groups * capacity).astype(jnp.int32)
     sources = jnp.zeros((2, cells), jnp.float32).at[:, target].add(values).reshape(2, sx, sy, sz)

time: 72.1 us -> 69.6 us (0.965)
  the two profiles are of different devices: /device:TPU:18 before, /device:TPU:10 now
where the time goes in v1:
time: 69.6 us; the launch traced here: 69 us
  starting transfers between devices  24.1 us (35%)
  other arithmetic  18.3 us (26%)
  local copies, waits for them, and re-layouts  15.7 us (23%)
  waiting for transfers between devices  9.83 us (14%)
  between operations  1.06 us (2%)
    slice x1, local copies, waits for them, and re-layouts, local(): sources[0]  12.3 us
    ppermute x4, starting transfers between devices, padded_2(): lax.ppermute(head, axis, [((i + 1) % count, i) for i in range(ends)])  10.4 us
    ppermute x4, starting transfers between devices, padded_2(): lax.ppermute(tail, axis, [(i, (i + 1) % count) for i in range(ends)])  10.2 us
    ppermute x4, waiting for transfers between devices, padded_2(): lax.ppermute(tail, axis, [(i, (i + 1) % count) for i in range(ends)])  9.52 us
    scatter-add x1, other arithmetic, local(): jnp.zeros((2, cells), jnp.float32).at[:, target].add(values)  5.81 us
    ppermute x3, starting transfers between devices, _press_racks(): k_now = ppermute(k_now, 'gx', sheets)  3.52 us
  transfers between devices with their start and end apart: 11, of which 4 were waited for; matrix products, arithmetic and copies ran while one was open for 32% of the time, Pallas kernels for 0%

profile of v1, /device:TPU:10, one launch (start us, length us, event | category | flops | bytes accessed | tf_op | source)
XLA Modules:
  0.0 69.0 jit_solution(16116015259104014786)
XLA Ops:
  0.6 0.0 copy-start
  0.6 0.7 %compare_select_fusion.1 = s32[2]{0:T(128)S(1)} fusion(s32[2]{0:T(128)} %param.25), kind=kLoop, calls=%fused_computation.299 | loop fusion | flops 6 | bytes 16 | tf_op jit(solution)/shard_map/jit(_take)/jit(_where)/select_n | solution.py:156
  1.4 0.7 compare_and_fusion
  2.0 0.7 %fusion.156 = s32[128,4]{1,0:T(8,128)S(1)} fusion(s32[128]{0:T(128)} %bitcast.77), kind=kLoop, calls=%fused_computation.286 | loop fusion | flops 1024 | bytes 2560 | tf_op jit(solution)/shard_map/convert_element_type | solution.py:159
  2.8 0.2 reduce_window_sum.11
  2.9 0.8 %select_reduce_fusion = s32[128]{0:T(128)S(1)} fusion(s32[128,4]{1,0:T(8,128)S(1)} %reduce_window_sum.11, s32[128]{0:T(128)} %bitcast.78), kind=kLoop, calls=%fused_computation.284 | loop fusion | flops 1408 | bytes 3072 | tf_op jit(solution)/shard_map/reduce_sum | solution.py:161
  3.8 0.7 fusion.159
  4.4 0.7 convert_bitcast_fusion
  5.1 0.6 gather_fusion
  5.7 0.1 broadcast_select_fusion
  5.8 0.1 copy.20
  5.9 0.9 %scatter_custom_fusion = f32[3,256]{0,1:T(8,128)S(1)} fusion(s32[128]{0:T(128)S(1)} %fusion.159, f32[128,3]{1,0:T(8,128)S(1)} %copy.20, f32[]{:T(128)} %constant.32.clone.1), kind=kCustom, calls=%fused_computation.287 | custom fusion | bytes 3076 | tf_op jit(solution)/shard_map/scatter | solution.py:164
  6.8 0.1 copy.28
  6.9 0.5 collective-permute-start.4
  7.4 0.1 copy.29
  7.4 2.6 %collective-permute-start.5 = (f32[3,1,64]{2,1,0:T(1,128)S(1)}, f32[3,1,64]{2,1,0:T(1,128)S(1)}, u32[]{:S(2)}, u32[]{:S(2)}) collective-permute-start(f32[3,1,64]{2,1,0:T(1,128)S(1)} %copy.29), channel_id=1, source_target_pairs={{0,8},{4,12},{8,0},{12,4},{1,9},{5,13},{9,1},{13,5},{2,10},{6,14},... | collective-permute-start | bytes 2312 | tf_op jit(solution)/shard_map/ppermute | solution.py:29
  10.0 0.1 copy.30
  10.1 0.5 collective-permute-start.6
  10.6 0.8 %fusion.152 = (f32[2,4,16,128]{3,2,1,0:T(8,128)S(1)}, f32[2,4,16,128]{3,2,1,0:T(8,128)S(1)}) fusion(f32[1,8,16,128]{3,2,1,0:T(8,128)} %bitcast.59, f32[1,8,16,128]{3,2,1,0:T(8,128)} %bitcast.47), kind=kLoop, calls=%fused_computation.259 | loop fusion | flops 32768 | bytes 262144 | tf_op jit(solution)/shard_map/stack | solution.py:170
  11.4 3.3 %collective-permute-start = (f32[2,4,16,128]{3,2,1,0:T(8,128)S(1)}, f32[2,4,16,128]{3,2,1,0:T(8,128)S(1)}, u32[]{:S(2)}, u32[]{:S(2)}) collective-permute-start(f32[2,4,16,128]{3,2,1,0:T(8,128)S(1)} %get-tuple-element.42), channel_id=1, source_target_pairs={{4,0},{8,4},{12,8},{5,1},{9,5},{13,9},{6,2},{10,6},{14,10},{7,3},{... | collective-permute-start | bytes 196616 | tf_op jit(solution)/shard_map/ppermute | solution.py:50
  14.6 2.6 %collective-permute-start.1 = (f32[2,4,16,128]{3,2,1,0:T(8,128)S(1)}, f32[2,4,16,128]{3,2,1,0:T(8,128)S(1)}, u32[]{:S(2)}, u32[]{:S(2)}) collective-permute-start(f32[2,4,16,128]{3,2,1,0:T(8,128)S(1)} %get-tuple-element.41), channel_id=1, source_target_pairs={{0,4},{4,8},{8,12},{1,5},{5,9},{9,13},{2,6},{6,10},{10,14},{3,7},{... | collective-permute-start | bytes 196616 | tf_op jit(solution)/shard_map/ppermute | solution.py:48
  17.2 1.1 %fusion.170 = (f32[8,16,128]{2,1,0:T(8,128)S(1)}, f32[8,16,128]{2,1,0:T(8,128)S(1)}) fusion(f32[8,16,128]{2,1,0:T(8,128)} %param.21), kind=kLoop, calls=%fused_computation.314 | loop fusion | bytes 196608 | tf_op jit(solution)/shard_map/sin | solution.py:103
  18.3 1.1 %fusion.160 = (f32[8,16,128]{2,1,0:T(8,128)S(1)}, f32[8,16,128]{2,1,0:T(8,128)S(1)}, f32[8,16,128]{2,1,0:T(8,128)S(1)}, f32[8,16,128]{2,1,0:T(8,128)S(1)}, f32[8...) fusion(f32[8,16,128]{2,1,0:T(8,128)S(1)} %get-tuple-element.48, f32[8,16,128]{2,1,0:T(8,128)} %param.22, ...), kind=kLoop, calls=%fused_computation.312 | loop fusion | flops 163840 | bytes 589824 | tf_op jit(solution)/shard_map/mul | solution.py:107
  19.4 0.1 copy.27
  19.5 0.0 collective-permute-done.4
  19.6 0.0 collective-permute-done.5
  19.6 0.0 collective-permute-done.6
  19.7 0.1 convert_element_type.37
  19.8 0.1 copy.26
  19.9 5.8 %scatter_custom_fusion.1 = f32[2,16384]{0,1:T(8,128)} fusion(s32[256]{0:T(256)S(1)} %bitcast.79, f32[256,2]{1,0:T(8,128)S(1)} %bitcast.76, f32[]{:T(128)} %constant.32.clone.1), kind=kCustom, calls=%fused_computation.5 | custom fusion | flops 512 | bytes 131076 | tf_op jit(solution)/shard_map/scatter-add | solution.py:169
  25.7 12.3 %slice_reduce_fusion.1 = (f32[16384]{0:T(1024)S(1)}, f32[16384]{0:T(1024)S(1)}) fusion(f32[2,16384]{0,1:T(8,128)} %scatter_custom_fusion.1), kind=kLoop, calls=%fused_computation.4 | loop fusion | bytes 262144 | tf_op jit(solution)/shard_map/slice | solution.py:172
  38.1 1.9 %collective-permute-start.2 = (f32[2,16,4,128]{3,2,1,0:T(4,128)S(1)}, f32[2,16,4,128]{3,2,1,0:T(4,128)S(1)}, u32[]{:S(2)}, u32[]{:S(2)}) collective-permute-start(f32[2,16,4,128]{3,2,1,0:T(4,128)S(1)} %get-tuple-element.27), channel_id=1, source_target_pairs={{1,0},{2,1},{3,2},{5,4},{6,5},{7,6},{9,8},{10,9},{11,10},{13,12},{... | collective-permute-start | bytes 196616 | tf_op jit(solution)/shard_map/ppermute | solution.py:50
  40.0 0.0 copy-start.5
  40.0 0.0 copy-start.6
  40.1 0.0 copy-start.8
  40.1 2.5 %collective-permute-start.3 = (f32[2,16,4,128]{3,2,1,0:T(4,128)S(1)}, f32[2,16,4,128]{3,2,1,0:T(4,128)S(1)}, u32[]{:S(2)}, u32[]{:S(2)}) collective-permute-start(f32[2,16,4,128]{3,2,1,0:T(4,128)S(1)} %get-tuple-element.26), channel_id=1, source_target_pairs={{0,1},{1,2},{2,3},{4,5},{5,6},{6,7},{8,9},{9,10},{10,11},{12,13},{... | collective-permute-start | bytes 196616 | tf_op jit(solution)/shard_map/ppermute | solution.py:48
  42.6 0.0 copy-start.7
  42.7 0.0 copy-start.9
  42.7 3.1 %collective-permute-done.3 = f32[2,16,4,128]{3,2,1,0:T(4,128)S(1)} collective-permute-done((f32[2,16,4,128]{3,2,1,0:T(4,128)S(1)}, f32[2,16,4,128]{3,2,1,0:T(4,128)S(1)}, u32[]{:S(2)}, u32[]{:S(2)}) %collective-permute-start.3) | collective-permute-done | bytes 65568 | tf_op jit(solution)/shard_map/ppermute | solution.py:48
  45.8 0.4 select_maximum_fusion.5
  46.2 0.4 fusion.39
  46.6 0.1 pad_maximum_fusion
  46.7 0.7 %fusion.18 = (f32[2,16,16,128]{3,2,1,0:T(8,128)S(1)}, f32[2,16,16,128]{3,2,1,0:T(8,128)S(1)}) fusion(f32[2,16,24,136]{3,2,1,0:T(8,128)S(1)} %select_maximum_fusion.5, f32[2,16,20,128]{3,2,1,0:T(8,128)S(1)} %get-tuple-element.25, f32[2,16,20,128]{3,2,1,0:T(8,128)S(1)} %get-tuple-element.24), kind=kLoop, calls=%fused_computation.48 | loop fusion | flops 1441792 | bytes 4718592 | tf_op jit(solution)/shard_map/add | solution.py:79
  47.4 0.6 fusion.101
  48.0 0.1 add_add_fusion.2
  48.0 0.0 copy-start.2
  48.1 0.1 add_add_fusion.3
  48.1 0.0 copy-start.4
  48.2 3.3 %collective-permute-start.7 = (f32[2,4,16,128]{3,2,1,0:T(8,128)S(1)}, f32[2,4,16,128]{3,2,1,0:T(8,128)S(1)}, u32[]{:S(2)}, u32[]{:S(2)}) collective-permute-start(f32[2,4,16,128]{3,2,1,0:T(8,128)S(1)} %get-tuple-element.33), channel_id=1, source_target_pairs={{4,0},{8,4},{12,8},{5,1},{9,5},{13,9},{6,2},{10,6},{14,10},{7,3},{... | collective-permute-start | bytes 196616 | tf_op jit(solution)/shard_map/ppermute | solution.py:50
  51.5 2.6 %collective-permute-start.8 = (f32[2,4,16,128]{3,2,1,0:T(8,128)S(1)}, f32[2,4,16,128]{3,2,1,0:T(8,128)S(1)}, u32[]{:S(2)}, u32[]{:S(2)}) collective-permute-start(f32[2,4,16,128]{3,2,1,0:T(8,128)S(1)} %get-tuple-element.32), channel_id=1, source_target_pairs={{0,4},{4,8},{8,12},{1,5},{5,9},{9,13},{2,6},{6,10},{10,14},{3,7},{... | collective-permute-start | bytes 196616 | tf_op jit(solution)/shard_map/ppermute | solution.py:48
  54.0 0.3 collective-permute-done.7
  54.3 3.3 %collective-permute-done.8 = f32[2,4,16,128]{3,2,1,0:T(8,128)S(1)} collective-permute-done((f32[2,4,16,128]{3,2,1,0:T(8,128)S(1)}, f32[2,4,16,128]{3,2,1,0:T(8,128)S(1)}, u32[]{:S(2)}, u32[]{:S(2)}) %collective-permute-start.8) | collective-permute-done | bytes 65568 | tf_op jit(solution)/shard_map/ppermute | solution.py:48
  57.7 1.9 %collective-permute-start.9 = (f32[2,16,4,128]{3,2,1,0:T(4,128)S(1)}, f32[2,16,4,128]{3,2,1,0:T(4,128)S(1)}, u32[]{:S(2)}, u32[]{:S(2)}) collective-permute-start(f32[2,16,4,128]{3,2,1,0:T(4,128)S(1)} %get-tuple-element.23), channel_id=1, source_target_pairs={{1,0},{2,1},{3,2},{5,4},{6,5},{7,6},{9,8},{10,9},{11,10},{13,12},{... | collective-permute-start | bytes 196616 | tf_op jit(solution)/shard_map/ppermute | solution.py:50
  59.6 0.0 copy-start.10
  59.6 2.5 %collective-permute-start.10 = (f32[2,16,4,128]{3,2,1,0:T(4,128)S(1)}, f32[2,16,4,128]{3,2,1,0:T(4,128)S(1)}, u32[]{:S(2)}, u32[]{:S(2)}) collective-permute-start(f32[2,16,4,128]{3,2,1,0:T(4,128)S(1)} %get-tuple-element.22), channel_id=1, source_target_pairs={{0,1},{1,2},{2,3},{4,5},{5,6},{6,7},{8,9},{9,10},{10,11},{12,13},{... | collective-permute-start | bytes 196616 | tf_op jit(solution)/shard_map/ppermute | solution.py:48
  62.2 3.1 %collective-permute-done.10 = f32[2,16,4,128]{3,2,1,0:T(4,128)S(1)} collective-permute-done((f32[2,16,4,128]{3,2,1,0:T(4,128)S(1)}, f32[2,16,4,128]{3,2,1,0:T(4,128)S(1)}, u32[]{:S(2)}, u32[]{:S(2)}) %collective-permute-start.10) | collective-permute-done | bytes 65568 | tf_op jit(solution)/shard_map/ppermute | solution.py:48
  65.3 0.4 select_maximum_fusion
  65.7 0.4 fusion.32
  66.1 0.5 fusion.4
  66.7 0.1 pad_maximum_fusion.1
  66.8 0.2 fusion.11
  67.0 0.6 fusion.50
  67.6 0.7 %fusion.155 = (f32[8,16,128]{2,1,0:T(8,128)}, f32[8,16,128]{2,1,0:T(8,128)}, f32[8,16,128]{2,1,0:T(8,128)S(1)}) fusion(f32[8,16,128]{2,1,0:T(8,128)S(1)} %add_add_fusion.3, bf16[2,8,16,128]{3,2,1,0:T(8,128)(2,1)S(1)} %copy-done.10, f32[8,16,128]{2,1,0:T(8,128)S(1)} %bitcast.73, f32[8,16,128]{2,1,0:T(8,128)S(1)} %copy-done.5, ...), kind=kLoop, calls=%fused_computation.279 | loop fusion | flops 327680 | bytes 983040 | tf_op jit(solution)/shard_map/add | solution.py:175
  68.3 0.7 add_add_fusion
  (33 shorter events, 0.4 us)
Async XLA Ops:
  0.6 4.5 %copy-start = (f32[1024,128]{1,0:T(8,128)S(1)}, f32[1024,128]{1,0:T(8,128)}, u32[]{:S(2)}) copy-start(f32[1024,128]{1,0:T(8,128)} %param.24) | copy-start | bytes 1572868
  6.9 12.6 %collective-permute-start.4 = (f32[3,1,64]{2,1,0:T(1,128)S(1)}, f32[3,1,64]{2,1,0:T(1,128)S(1)}, u32[]{:S(2)}, u32[]{:S(2)}) collective-permute-start(f32[3,1,64]{2,1,0:T(1,128)S(1)} %copy.28), channel_id=1, source_target_pairs={{0,4},{4,0},{8,12},{12,8},{1,5},{5,1},{9,13},{13,9},{2,6},{6,2},{1... | collective-permute-start | bytes 2312 | tf_op jit(solution)/shard_map/ppermute | solution.py:29
  7.4 12.2 %collective-permute-start.5 = (f32[3,1,64]{2,1,0:T(1,128)S(1)}, f32[3,1,64]{2,1,0:T(1,128)S(1)}, u32[]{:S(2)}, u32[]{:S(2)}) collective-permute-start(f32[3,1,64]{2,1,0:T(1,128)S(1)} %copy.29), channel_id=1, source_target_pairs={{0,8},{4,12},{8,0},{12,4},{1,9},{5,13},{9,1},{13,5},{2,10},{6,14},... | collective-permute-start | bytes 2312 | tf_op jit(solution)/shard_map/ppermute | solution.py:29
  10.1 9.5 %collective-permute-start.6 = (f32[3,1,64]{2,1,0:T(1,128)S(1)}, f32[3,1,64]{2,1,0:T(1,128)S(1)}, u32[]{:S(2)}, u32[]{:S(2)}) collective-permute-start(f32[3,1,64]{2,1,0:T(1,128)S(1)} %copy.30), channel_id=1, source_target_pairs={{0,12},{4,8},{8,4},{12,0},{1,13},{5,9},{9,5},{13,1},{2,14},{6,10},... | collective-permute-start | bytes 2312 | tf_op jit(solution)/shard_map/ppermute | solution.py:29
  11.4 26.6 %collective-permute-start = (f32[2,4,16,128]{3,2,1,0:T(8,128)S(1)}, f32[2,4,16,128]{3,2,1,0:T(8,128)S(1)}, u32[]{:S(2)}, u32[]{:S(2)}) collective-permute-start(f32[2,4,16,128]{3,2,1,0:T(8,128)S(1)} %get-tuple-element.42), channel_id=1, source_target_pairs={{4,0},{8,4},{12,8},{5,1},{9,5},{13,9},{6,2},{10,6},{14,10},{7,3},{... | collective-permute-start | bytes 196616 | tf_op jit(solution)/shard_map/ppermute | solution.py:50
  14.6 23.4 %collective-permute-start.1 = (f32[2,4,16,128]{3,2,1,0:T(8,128)S(1)}, f32[2,4,16,128]{3,2,1,0:T(8,128)S(1)}, u32[]{:S(2)}, u32[]{:S(2)}) collective-permute-start(f32[2,4,16,128]{3,2,1,0:T(8,128)S(1)} %get-tuple-element.41), channel_id=1, source_target_pairs={{0,4},{4,8},{8,12},{1,5},{5,9},{9,13},{2,6},{6,10},{10,14},{3,7},{... | collective-permute-start | bytes 196616 | tf_op jit(solution)/shard_map/ppermute | solution.py:48
  25.7 12.3 %copy-start.1 = (f32[8,16,128]{2,1,0:T(8,128)S(1)}, f32[8,16,128]{2,1,0:T(8,128)}, u32[]{:S(2)}) copy-start(f32[8,16,128]{2,1,0:T(8,128)} %param.15) | copy-start | bytes 196612
  25.7 12.3 %copy-start.3 = (f32[8,16,128]{2,1,0:T(8,128)S(1)}, f32[8,16,128]{2,1,0:T(8,128)}, u32[]{:S(2)}) copy-start(f32[8,16,128]{2,1,0:T(8,128)} %param.14) | copy-start | bytes 196612
  38.1 4.6 %collective-permute-start.2 = (f32[2,16,4,128]{3,2,1,0:T(4,128)S(1)}, f32[2,16,4,128]{3,2,1,0:T(4,128)S(1)}, u32[]{:S(2)}, u32[]{:S(2)}) collective-permute-start(f32[2,16,4,128]{3,2,1,0:T(4,128)S(1)} %get-tuple-element.27), channel_id=1, source_target_pairs={{1,0},{2,1},{3,2},{5,4},{6,5},{7,6},{9,8},{10,9},{11,10},{13,12},{... | collective-permute-start | bytes 196616 | tf_op jit(solution)/shard_map/ppermute | solution.py:50
  40.0 7.9 %copy-start.5 = (f32[8,16,128]{2,1,0:T(8,128)S(1)}, f32[8,16,128]{2,1,0:T(8,128)}, u32[]{:S(2)}) copy-start(f32[8,16,128]{2,1,0:T(8,128)} %param.18) | copy-start | bytes 196612
  40.0 7.9 %copy-start.6 = (f32[8,16,128]{2,1,0:T(8,128)S(1)}, f32[8,16,128]{2,1,0:T(8,128)}, u32[]{:S(2)}) copy-start(f32[8,16,128]{2,1,0:T(8,128)} %param.20) | copy-start | bytes 196612
  40.1 7.9 %copy-start.8 = (f32[8,16,128]{2,1,0:T(8,128)S(1)}, f32[8,16,128]{2,1,0:T(8,128)}, u32[]{:S(2)}) copy-start(f32[8,16,128]{2,1,0:T(8,128)} %param.17) | copy-start | bytes 196612
  40.1 5.7 %collective-permute-start.3 = (f32[2,16,4,128]{3,2,1,0:T(4,128)S(1)}, f32[2,16,4,128]{3,2,1,0:T(4,128)S(1)}, u32[]{:S(2)}, u32[]{:S(2)}) collective-permute-start(f32[2,16,4,128]{3,2,1,0:T(4,128)S(1)} %get-tuple-element.26), channel_id=1, source_target_pairs={{0,1},{1,2},{2,3},{4,5},{5,6},{6,7},{8,9},{9,10},{10,11},{12,13},{... | collective-permute-start | bytes 196616 | tf_op jit(solution)/shard_map/ppermute | solution.py:48
  42.6 5.4 %copy-start.7 = (f32[8,16,128]{2,1,0:T(8,128)S(1)}, f32[8,16,128]{2,1,0:T(8,128)}, u32[]{:S(2)}) copy-start(f32[8,16,128]{2,1,0:T(8,128)} %param.19) | copy-start | bytes 196612
  42.7 5.4 %copy-start.9 = (f32[8,16,128]{2,1,0:T(8,128)S(1)}, f32[8,16,128]{2,1,0:T(8,128)}, u32[]{:S(2)}) copy-start(f32[8,16,128]{2,1,0:T(8,128)} %param.16) | copy-start | bytes 196612
  48.0 20.2 %copy-start.2 = (f32[8,16,128]{2,1,0:T(8,128)}, f32[8,16,128]{2,1,0:T(8,128)S(1)}, u32[]{:S(2)}) copy-start(f32[8,16,128]{2,1,0:T(8,128)S(1)} %get-tuple-element.14) | copy-start | bytes 196612
  48.1 19.4 %copy-start.4 = (f32[8,16,128]{2,1,0:T(8,128)}, f32[8,16,128]{2,1,0:T(8,128)S(1)}, u32[]{:S(2)}) copy-start(f32[8,16,128]{2,1,0:T(8,128)S(1)} %add_add_fusion.3) | copy-start | bytes 196612
  48.2 6.2 %collective-permute-start.7 = (f32[2,4,16,128]{3,2,1,0:T(8,128)S(1)}, f32[2,4,16,128]{3,2,1,0:T(8,128)S(1)}, u32[]{:S(2)}, u32[]{:S(2)}) collective-permute-start(f32[2,4,16,128]{3,2,1,0:T(8,128)S(1)} %get-tuple-element.33), channel_id=1, source_target_pairs={{4,0},{8,4},{12,8},{5,1},{9,5},{13,9},{6,2},{10,6},{14,10},{7,3},{... | collective-permute-start | bytes 196616 | tf_op jit(solution)/shard_map/ppermute | solution.py:50
  51.5 6.2 %collective-permute-start.8 = (f32[2,4,16,128]{3,2,1,0:T(8,128)S(1)}, f32[2,4,16,128]{3,2,1,0:T(8,128)S(1)}, u32[]{:S(2)}, u32[]{:S(2)}) collective-permute-start(f32[2,4,16,128]{3,2,1,0:T(8,128)S(1)} %get-tuple-element.32), channel_id=1, source_target_pairs={{0,4},{4,8},{8,12},{1,5},{5,9},{9,13},{2,6},{6,10},{10,14},{3,7},{... | collective-permute-start | bytes 196616 | tf_op jit(solution)/shard_map/ppermute | solution.py:48
  57.7 4.5 %collective-permute-start.9 = (f32[2,16,4,128]{3,2,1,0:T(4,128)S(1)}, f32[2,16,4,128]{3,2,1,0:T(4,128)S(1)}, u32[]{:S(2)}, u32[]{:S(2)}) collective-permute-start(f32[2,16,4,128]{3,2,1,0:T(4,128)S(1)} %get-tuple-element.23), channel_id=1, source_target_pairs={{1,0},{2,1},{3,2},{5,4},{6,5},{7,6},{9,8},{10,9},{11,10},{13,12},{... | collective-permute-start | bytes 196616 | tf_op jit(solution)/shard_map/ppermute | solution.py:50
  59.6 8.0 %copy-start.10 = (bf16[2,8,16,128]{3,2,1,0:T(8,128)(2,1)S(1)}, bf16[2,8,16,128]{3,2,1,0:T(8,128)(2,1)}, u32[]{:S(2)}) copy-start(bf16[2,8,16,128]{3,2,1,0:T(8,128)(2,1)} %param.23) | copy-start | bytes 196612
  59.6 5.7 %collective-permute-start.10 = (f32[2,16,4,128]{3,2,1,0:T(4,128)S(1)}, f32[2,16,4,128]{3,2,1,0:T(4,128)S(1)}, u32[]{:S(2)}, u32[]{:S(2)}) collective-permute-start(f32[2,16,4,128]{3,2,1,0:T(4,128)S(1)} %get-tuple-element.22), channel_id=1, source_target_pairs={{0,1},{1,2},{2,3},{4,5},{5,6},{6,7},{8,9},{9,10},{10,11},{12,13},{... | collective-permute-start | bytes 196616 | tf_op jit(solution)/shard_map/ppermute | solution.py:48
